TPU v7x, 32 devices: a whole 2x2x4 slice. The times are simulated.
32 devices in a mesh: dp: 8 (over y, x, core), fsdp: 4 (over z).
Axes of the slice: x: 2, y: 2, z: 4, core: 2. Of those that a mesh axis runs over, the one named last changes fastest.
Arguments:
- tokens: bfloat16 [18432, 768], P(('dp', 'fsdp')), may hold values from -6 to 6
- image_lengths: int32 [32, 9], P(('dp', 'fsdp')), may hold values from 0 to 576, as said below
- w_qkv: bfloat16 [768, 2304], P('fsdp'), may hold values from -0.21875 to 0.21875
- w_out: bfloat16 [768, 768], P('fsdp'), may hold values from -0.875 to 0.875
- w_up: bfloat16 [768, 3072], P('fsdp'), may hold values from -0.21875 to 0.21875
- w_down: bfloat16 [3072, 768], P('fsdp'), may hold values from -0.109375 to 0.109375
- ln_gain: bfloat16 [2, 768], P(None, 'fsdp'), may hold values from 0.25 to 1.75
- ln_bias: bfloat16 [2, 768], P(None, 'fsdp'), may hold values from -3 to 3
- qk_gain: bfloat16 [2, 768], P(None, 'fsdp'), may hold values from 0.25 to 1.75
- cotangent: bfloat16 [18432, 768], P(('dp', 'fsdp')), may hold values from -6 to 6
Outputs:
- layer_out: bfloat16 [18432, 768], P(('dp', 'fsdp'))
- grad_tokens: bfloat16 [18432, 768], P(('dp', 'fsdp'))
- grad_w_qkv: float32 [768, 2304], P('fsdp')
- grad_w_out: float32 [768, 768], P('fsdp')
- grad_w_up: float32 [768, 3072], P('fsdp')
- grad_w_down: float32 [3072, 768], P('fsdp')
- grad_ln_gain: float32 [2, 768], P(None, 'fsdp')
- grad_ln_bias: float32 [2, 768], P(None, 'fsdp')
- grad_qk_gain: float32 [2, 768], P(None, 'fsdp')
Inputs may be any that keep to these rules, and one draw needn't show every extreme that they name: Each row of image_lengths is either 1 large images of 576 patches, or between 1 and 9 small images of 64 patches; used slots come first, zeros after. Exactly half of the rows hold large images. No image crosses a multiple of 576 rows, and padding lies after the last image.
All inputs are finite; a program needn't handle non-finite values.
Results may differ from a plain program's by a relative error of at most 0.02.
Values may be sent and summed in bfloat16 or wider, within the bound.
No kernel may reach another device: no remote copies, remote signals or barrier semaphores. Data moves between devices by JAX's collectives and lax.ppermute only.
A program may use at most 192 MiB of HBM per device.

v0:
```python
from functools import partial
import jax
import jax.numpy as jnp
from jax import lax
from jax.sharding import PartitionSpec as P

HEADS = 12
HEAD_DIM = 64
PATCH_BIG = 576
epsilon = 1e-06


def layer_norm(v, gain_row, bias_row):
    centre = v - jnp.mean(v, axis=-1, keepdims=True)
    spread = jnp.mean(centre * centre, axis=-1, keepdims=True)
    return centre * lax.rsqrt(spread + epsilon) * gain_row + bias_row


def head_norm(v, gain_row):
    centre = v - jnp.mean(v, axis=-1, keepdims=True)
    spread = jnp.mean(centre * centre, axis=-1, keepdims=True)
    return centre * lax.rsqrt(spread + epsilon) * gain_row


def both_norms(q_in, k_in, q_gain, k_gain):
    return (head_norm(q_in, q_gain), head_norm(k_in, k_gain))


def on_device(
    tokens, image_lengths, w_qkv, w_out, w_up, w_down, ln_gain, ln_bias, qk_gain, cotangent
):
    full_qkv, full_out, full_up, full_down, gain_all, bias_all, qk_all = (
        lax.all_gather(w_qkv, "fsdp", axis=0, tiled=True),
        lax.all_gather(w_out, "fsdp", axis=0, tiled=True),
        lax.all_gather(w_up, "fsdp", axis=0, tiled=True),
        lax.all_gather(w_down, "fsdp", axis=0, tiled=True),
        lax.all_gather(ln_gain, "fsdp", axis=1, tiled=True),
        lax.all_gather(ln_bias, "fsdp", axis=1, tiled=True),
        lax.all_gather(qk_gain, "fsdp", axis=1, tiled=True),
    )
    length = tokens.shape[0]
    model_width = tokens.shape[1]
    blocks = length // PATCH_BIG
    scaling = HEAD_DIM ** (-0.5)
    position = jnp.arange(length, dtype=jnp.int32)
    limits = jnp.cumsum(image_lengths[0])
    segment = jnp.sum((position[:, None] >= limits[None, :]).astype(jnp.int32), axis=1)
    valid_rows = (position < limits[-1]).astype(jnp.float32)[:, None]
    norm_gains = gain_all.astype(jnp.float32)
    biases = bias_all.astype(jnp.float32)
    qk_gains = qk_all.astype(jnp.float32).reshape(2, HEADS, HEAD_DIM)
    inputs = tokens.astype(jnp.float32)
    normed, first_back = jax.vjp(layer_norm, inputs, norm_gains[0], biases[0])
    normed_low = normed.astype(jnp.bfloat16)
    project = jnp.dot(normed_low, full_qkv, preferred_element_type=jnp.float32)
    queries = project[:, :model_width].reshape(length, HEADS, HEAD_DIM)
    keys_raw = project[:, model_width : 2 * model_width].reshape(length, HEADS, HEAD_DIM)
    values_raw = project[:, 2 * model_width :]
    (q_norm, k_norm), norms_back = jax.vjp(both_norms, queries, keys_raw, qk_gains[0], qk_gains[1])
    q_low = q_norm.astype(jnp.bfloat16).reshape(blocks, PATCH_BIG, HEADS, HEAD_DIM)
    k_low = k_norm.astype(jnp.bfloat16).reshape(blocks, PATCH_BIG, HEADS, HEAD_DIM)
    v_low = values_raw.astype(jnp.bfloat16).reshape(blocks, PATCH_BIG, HEADS, HEAD_DIM)
    s_blocks = segment.reshape(blocks, PATCH_BIG)

    def block_scores(q_block, k_block, s_block):
        scores = (
            jnp.einsum("qhd,khd->hqk", q_block, k_block, preferred_element_type=jnp.float32)
            * scaling
        )
        return jnp.where((s_block[:, None] == s_block[None, :])[None], scores, -1e30)

    def attend(members):
        q_block, k_block, v_block, s_block = members
        scores = block_scores(q_block, k_block, s_block)
        row_top = jnp.max(scores, axis=-1, keepdims=True)
        exp_scores = jnp.exp(scores - row_top)
        row_total = jnp.sum(exp_scores, axis=-1, keepdims=True)
        probability = (exp_scores / row_total).astype(jnp.bfloat16)
        mixed_block = jnp.einsum(
            "hqk,khd->qhd", probability, v_block, preferred_element_type=jnp.float32
        )
        return (mixed_block, row_top + jnp.log(row_total))

    mixed_heads, log_total = lax.map(attend, (q_low, k_low, v_low, s_blocks))
    mixed_low = mixed_heads.reshape(length, model_width).astype(jnp.bfloat16)
    residual = inputs + jnp.dot(mixed_low, full_out, preferred_element_type=jnp.float32)
    second, second_back = jax.vjp(layer_norm, residual, norm_gains[1], biases[1])
    second_low = second.astype(jnp.bfloat16)
    up_pre = jnp.dot(second_low, full_up, preferred_element_type=jnp.float32)
    active, gelu_back = jax.vjp(partial(jax.nn.gelu, approximate=False), up_pre)
    active_low = active.astype(jnp.bfloat16)
    output = residual + jnp.dot(active_low, full_down, preferred_element_type=jnp.float32)
    layer_out = (valid_rows * output).astype(jnp.bfloat16)
    back_qkv, back_out, back_up, back_down = (
        lax.all_gather(w_qkv, "fsdp", axis=0, tiled=True),
        lax.all_gather(w_out, "fsdp", axis=0, tiled=True),
        lax.all_gather(w_up, "fsdp", axis=0, tiled=True),
        lax.all_gather(w_down, "fsdp", axis=0, tiled=True),
    )
    upstream = cotangent.astype(jnp.float32) * valid_rows
    up_low = upstream.astype(jnp.bfloat16)
    grad_down = jnp.dot(active_low.T, up_low, preferred_element_type=jnp.float32)
    grad_active = jnp.dot(up_low, back_down.T, preferred_element_type=jnp.float32)
    (grad_pre,) = gelu_back(grad_active)
    pre_low = grad_pre.astype(jnp.bfloat16)
    grad_up = jnp.dot(second_low.T, pre_low, preferred_element_type=jnp.float32)
    grad_second = jnp.dot(pre_low, back_up.T, preferred_element_type=jnp.float32)
    grad_resid, gain_two, bias_two = second_back(grad_second)
    grad_resid = grad_resid + upstream
    resid_low = grad_resid.astype(jnp.bfloat16)
    grad_outw = jnp.dot(mixed_low.T, resid_low, preferred_element_type=jnp.float32)
    grad_mixed = jnp.dot(resid_low, back_out.T, preferred_element_type=jnp.float32)
    grad_mixed = grad_mixed.astype(jnp.bfloat16).reshape(blocks, PATCH_BIG, HEADS, HEAD_DIM)

    def attend_back(members):
        q_block, k_block, v_block, s_block, l_block, d_block = members
        scores = block_scores(q_block, k_block, s_block)
        probability = jnp.exp(scores - l_block)
        prob_low = probability.astype(jnp.bfloat16)
        grad_v = jnp.einsum("hqk,qhd->khd", prob_low, d_block, preferred_element_type=jnp.float32)
        grad_p = jnp.einsum("qhd,khd->hqk", d_block, v_block, preferred_element_type=jnp.float32)
        grad_p = lax.optimization_barrier(grad_p.astype(jnp.bfloat16)).astype(jnp.float32)
        grad_s = probability * (grad_p - jnp.sum(probability * grad_p, axis=-1, keepdims=True))
        s_low = grad_s.astype(jnp.bfloat16)
        grad_q = (
            jnp.einsum("hqk,khd->qhd", s_low, k_block, preferred_element_type=jnp.float32) * scaling
        )
        grad_k = (
            jnp.einsum("hqk,qhd->khd", s_low, q_block, preferred_element_type=jnp.float32) * scaling
        )
        return (grad_q, grad_k, grad_v)

    grad_qn, grad_kn, grad_vn = lax.map(
        attend_back, (q_low, k_low, v_low, s_blocks, log_total, grad_mixed)
    )
    grad_q, grad_k, gain_q, gain_k = norms_back(
        (grad_qn.reshape(length, HEADS, HEAD_DIM), grad_kn.reshape(length, HEADS, HEAD_DIM))
    )
    grad_project = jnp.concatenate(
        [
            grad_q.reshape(length, model_width),
            grad_k.reshape(length, model_width),
            grad_vn.reshape(length, model_width),
        ],
        axis=1,
    ).astype(jnp.bfloat16)
    grad_qkv = jnp.dot(normed_low.T, grad_project, preferred_element_type=jnp.float32)
    grad_normed = jnp.dot(grad_project, back_qkv.T, preferred_element_type=jnp.float32)
    grad_input, gain_one, bias_one = first_back(grad_normed)
    grad_tokens = (grad_input + grad_resid).astype(jnp.bfloat16)
    grad_gain = jnp.stack([gain_one, gain_two])
    grad_bias = jnp.stack([bias_one, bias_two])
    grad_qk = jnp.stack([gain_q.reshape(model_width), gain_k.reshape(model_width)])
    summands = (grad_qkv, grad_outw, grad_up, grad_down, grad_gain, grad_bias, grad_qk)
    pieces = (
        lax.psum_scatter(
            summands[0].astype(jnp.bfloat16), "fsdp", scatter_dimension=0, tiled=True
        ).astype(jnp.float32),
        lax.psum_scatter(
            summands[1].astype(jnp.bfloat16), "fsdp", scatter_dimension=0, tiled=True
        ).astype(jnp.float32),
        lax.psum_scatter(
            summands[2].astype(jnp.bfloat16), "fsdp", scatter_dimension=0, tiled=True
        ).astype(jnp.float32),
        lax.psum_scatter(
            summands[3].astype(jnp.bfloat16), "fsdp", scatter_dimension=0, tiled=True
        ).astype(jnp.float32),
        lax.psum_scatter(
            summands[4].astype(jnp.bfloat16), "fsdp", scatter_dimension=1, tiled=True
        ).astype(jnp.float32),
        lax.psum_scatter(
            summands[5].astype(jnp.bfloat16), "fsdp", scatter_dimension=1, tiled=True
        ).astype(jnp.float32),
        lax.psum_scatter(
            summands[6].astype(jnp.bfloat16), "fsdp", scatter_dimension=1, tiled=True
        ).astype(jnp.float32),
    )
    shares = (
        lax.psum(pieces[0].astype(jnp.bfloat16), "dp").astype(jnp.float32),
        lax.psum(pieces[1].astype(jnp.bfloat16), "dp").astype(jnp.float32),
        lax.psum(pieces[2].astype(jnp.bfloat16), "dp").astype(jnp.float32),
        lax.psum(pieces[3].astype(jnp.bfloat16), "dp").astype(jnp.float32),
        lax.psum(pieces[4].astype(jnp.bfloat16), "dp").astype(jnp.float32),
        lax.psum(pieces[5].astype(jnp.bfloat16), "dp").astype(jnp.float32),
        lax.psum(pieces[6].astype(jnp.bfloat16), "dp").astype(jnp.float32),
    )
    return (
        layer_out,
        grad_tokens,
        shares[0],
        shares[1],
        shares[2],
        shares[3],
        shares[4],
        shares[5],
        shares[6],
    )


def solution(mesh):
    in_specs = (
        P(("dp", "fsdp"), None),
        P(("dp", "fsdp"), None),
        P("fsdp", None),
        P("fsdp", None),
        P("fsdp", None),
        P("fsdp", None),
        P(None, "fsdp"),
        P(None, "fsdp"),
        P(None, "fsdp"),
        P(("dp", "fsdp"), None),
    )
    out_specs = (
        P(("dp", "fsdp"), None),
        P(("dp", "fsdp"), None),
        P("fsdp", None),
        P("fsdp", None),
        P("fsdp", None),
        P("fsdp", None),
        P(None, "fsdp"),
        P(None, "fsdp"),
        P(None, "fsdp"),
    )
    return jax.shard_map(
        on_device, mesh=mesh, in_specs=in_specs, out_specs=out_specs, check_vma=False
    )
```

profile of v0, /device:TPU:0, one launch (start us, length us, event | category | flops | bytes accessed | tf_op | source)
XLA Modules:
  0.0 768.0 jit_solution(16090609015939321576)
XLA Ops:
  11.6 12.7 %all-gather = bf16[4,192,2]{1,2,0:T(2,128)(2,1)S(1)} all-gather(bf16[1,192,2]{1,2,0:T(2,128)(2,1)S(1)} %bitcast.126), channel_id=1, replica_groups=mesh['dp'=8,'fsdp'=4] {'fsdp'}, dimensions={0}, use_global_device_ids=true | all-gather | bytes 3840 | tf_op jit(solution)/shard_map/all_gather | solution.py:37
  24.4 8.1 %all-gather.1 = bf16[4,192,2]{1,2,0:T(2,128)(2,1)S(1)} all-gather(bf16[1,192,2]{1,2,0:T(2,128)(2,1)S(1)} %bitcast.127), channel_id=1, replica_groups=mesh['dp'=8,'fsdp'=4] {'fsdp'}, dimensions={0}, use_global_device_ids=true | all-gather | bytes 3840 | tf_op jit(solution)/shard_map/all_gather | solution.py:38
  32.5 10.7 %all-gather.2 = bf16[4,192,2]{1,2,0:T(2,128)(2,1)S(1)} all-gather(bf16[1,192,2]{1,2,0:T(2,128)(2,1)S(1)} %bitcast.128), channel_id=1, replica_groups=mesh['dp'=8,'fsdp'=4] {'fsdp'}, dimensions={0}, use_global_device_ids=true | all-gather | bytes 3840 | tf_op jit(solution)/shard_map/all_gather | solution.py:39
  44.5 37.8 %all-gather.8.cloned.1.call-done = bf16[768,2304]{1,0:T(8,128)(2,1)} async-done(((bf16[192,2304]{1,0:T(8,128)(2,1)}), bf16[768,2304]{1,0:T(8,128)(2,1)}) %all-gather.8.cloned.1.call-update) | async-done | bytes 3538960 | tf_op jit(solution)/shard_map/all_gather | solution.py:33
  82.3 4.4 fusion.54
  86.9 2.0 fusion.61
  88.9 1.5 copy.68
  90.4 1.9 copy.71
  92.7 2.8 copy.69
  95.5 1.7 reduce_sum.228
  97.2 2.0 multiply_reduce_fusion.1
  99.4 8.1 %fusion.62 = (f32[12,576]{1,0:T(8,128)S(1)}, f32[12,576,576]{1,2,0:T(8,128)}) fusion(f32[576,12,64]{0,2,1:T(8,128)S(1)} %bitcast.95, f32[12,64]{1,0:T(8,128)S(1)} %mul.324, f32[576,12]{0,1:T(8,128)S(1)} %fusion.47, f32[576,12]{0,1:T(8,128)S(1)} %broadcast_multiply_fusion, f32[576,12,64]{0,2,1:T(8,128)S(1)} %bitcast.102, f32[12,64]{1,0:T(8,128)S(1)} %mul.318, ...), kind=kOutput, calls=%fused_computation.139 | convolution fusion | flops 525083904 | bytes 19940352 | tf_op jit(solution)/shard_map/while/body/eval_jaxpr/qhd,khd->hqk/dot_general | solution.py:67
  107.5 8.5 %fusion.3 = f32[12,576]{1,0:T(8,128)S(1)} fusion(f32[12,576,576]{1,2,0:T(8,128)} %get-tuple-element.91, f32[12,576]{1,0:T(8,128)S(1)} %get-tuple-element.90), kind=kLoop, calls=%fused_computation.9 | loop fusion | flops 7955712 | bytes 15980544 | tf_op jit(solution)/shard_map/while/body/eval_jaxpr/reduce_sum | solution.py:77
  116.0 11.4 %fusion.31 = bf16[12,64,576]{2,1,0:T(8,128)(2,1)} fusion(bf16[576,12,64]{0,2,1:T(8,128)(2,1)} %bitcast.109, f32[12,576,576]{1,2,0:T(8,128)} %get-tuple-element.91, f32[12,576]{1,0:T(8,128)S(1)} %fusion.3, f32[12,576]{1,0:T(8,128)S(1)} %get-tuple-element.90), kind=kOutput, calls=%fused_computation.81 | convolution fusion | flops 521994240 | bytes 17750016 | tf_op jit(solution)/shard_map/while/body/eval_jaxpr/hqk,khd->qhd/dot_general | solution.py:79
  127.4 2.6 fusion.63
  131.5 71.6 %all-gather.12.cloned.1.call-done = bf16[768,3072]{1,0:T(8,128)(2,1)} async-done(((bf16[192,3072]{1,0:T(8,128)(2,1)}), bf16[768,3072]{1,0:T(8,128)(2,1)}) %all-gather.12.cloned.1.call-update) | async-done | bytes 4718608 | tf_op jit(solution)/shard_map/all_gather | solution.py:35
  203.1 22.8 %multiply_convert_fusion = (bf16[576,3072]{1,0:T(8,128)(2,1)}, f32[576,3072]{1,0:T(8,128)}, f32[576,3072]{1,0:T(8,128)}) fusion(bf16[768,3072]{1,0:T(8,128)(2,1)} %all-gather.12.cloned.1.call-done, f32[576,768]{1,0:T(8,128)} %copy-done.7, f32[768]{0:T(1024)S(1)} %get-tuple-element.73, f32[768]{0:T(1024)S(1)} %get-tuple-element.102, f32[576]{0:T(1024)S(1)} %fusion.50, ...), kind=kOutput, calls=%fused_computation.17 | convolution fusion | flops 2835136512 | bytes 24193536 | tf_op jit(solution)/shard_map/dot_general | solution.py:89
  225.8 66.5 %all-gather.14.cloned.1.call-done = bf16[3072,768]{1,0:T(8,128)(2,1)} async-done(((bf16[768,768]{1,0:T(8,128)(2,1)}), bf16[3072,768]{1,0:T(8,128)(2,1)}) %all-gather.14.cloned.1.call-update) | async-done | bytes 4718608 | tf_op jit(solution)/shard_map/all_gather | solution.py:36
  292.4 11.3 %add_convert_fusion = bf16[576,3072]{1,0:T(8,128)(2,1)S(1)} fusion(f32[576,3072]{1,0:T(8,128)} %get-tuple-element.87, f32[576,3072]{1,0:T(8,128)} %get-tuple-element.94, bf16[3072,768]{1,0:T(8,128)(2,1)} %all-gather.14.cloned.1.call-done, bf16[576,768]{1,0:T(8,128)(2,1)} %param.19, f32[576]{0:T(1024)S(1)} %fusion.48), kind=kOutput, calls=%fused_computation.16 | convolution fusion | flops 2744008704 | bytes 23300352 | tf_op jit(solution)/shard_map/dot_general | solution.py:103
  303.7 3.3 multiply_reduce_fusion.2
  310.2 2.1 convolution_convert_fusion.4
  312.4 3.3 convolution_convert_fusion.5
  315.8 2.4 copy.73
  318.2 7.6 convolution_convert_fusion
  325.8 12.0 %fusion = f32[12,576]{1,0:T(8,128)S(1)} fusion(bf16[12,576,576]{1,2,0:T(8,128)(2,1)} %convolution_convert_fusion, f32[12,576,576]{1,2,0:T(8,128)} %get-tuple-element.91, f32[12,576]{1,0:T(8,128)S(1)} %log_add_fusion), kind=kLoop, calls=%fused_computation.2 | loop fusion | flops 15918336 | bytes 23943168 | tf_op jit(solution)/shard_map/while/body/eval_jaxpr/reduce_sum | solution.py:123
  338.3 6.6 fusion.2
  345.0 4.0 fusion.23
  349.0 1.8 fusion.24
  356.0 9.2 %fusion.32 = bf16[12,64,576]{2,1,0:T(8,128)(2,1)S(1)} fusion(bf16[576,12,64]{0,2,1:T(8,128)(2,1)S(1)} %bitcast.108, f32[12,576,576]{1,2,0:T(8,128)} %get-tuple-element.91, f32[12,576]{1,0:T(8,128)S(1)} %log_add_fusion), kind=kOutput, calls=%fused_computation.82 | convolution fusion | flops 518012928 | bytes 17722368 | tf_op jit(solution)/shard_map/while/body/eval_jaxpr/hqk,qhd->khd/dot_general | solution.py:120
  366.1 7.4 convolution_convert_fusion.1
  373.5 1.4 copy-done.9
  374.9 7.8 %convolution_convert_fusion.3 = bf16[768,3072]{1,0:T(8,128)(2,1)} fusion(bf16[576,3072]{1,0:T(8,128)(2,1)} %copy-done.38, f32[576,768]{1,0:T(8,128)S(1)} %copy-done.9, f32[768]{0:T(1024)S(1)} %get-tuple-element.73, f32[768]{0:T(1024)S(1)} %get-tuple-element.102, f32[576]{0:T(1024)S(1)} %fusion.50, f32[576]{0:T(1024)S(1)} %broadcast_multiply_fusion.4), kind=kOutput, calls=%fused_computation.34 | convolution fusion | flops 2722480128 | bytes 10037760 | tf_op jit(solution)/shard_map/dot_general | solution.py:106
  383.9 8.0 %convolution_convert_fusion.2 = bf16[3072,768]{1,0:T(8,128)(2,1)} fusion(bf16[576,3072]{1,0:T(8,128)(2,1)} %get-tuple-element.86, bf16[576,768]{1,0:T(8,128)(2,1)S(1)} %copy-done.13, f32[576]{0:T(1024)S(1)} %fusion.48), kind=kOutput, calls=%fused_computation.33 | convolution fusion | flops 2721595392 | bytes 9144576 | tf_op jit(solution)/shard_map/dot_general | solution.py:102
  393.4 5.0 fusion.58
  403.6 35.1 %reduce-scatter.14.cloned.1.call-done = bf16[192,2304]{1,0:T(8,128)(2,1)} async-done(((bf16[768,2304]{1,0:T(8,128)(2,1)}), bf16[192,2304]{1,0:T(8,128)(2,1)}) %reduce-scatter.14.cloned.1.call-update) | async-done | bytes 884752 | tf_op jit(solution)/shard_map/reduce_scatter | solution.py:156
  438.6 87.8 %reduce-scatter.18.cloned.1.call-done = bf16[192,3072]{1,0:T(8,128)(2,1)} async-done(((bf16[768,3072]{1,0:T(8,128)(2,1)}), bf16[192,3072]{1,0:T(8,128)(2,1)}) %reduce-scatter.18.cloned.1.call-update) | async-done | bytes 1179664 | tf_op jit(solution)/shard_map/reduce_scatter | solution.py:162
  526.4 88.1 %reduce-scatter.20.cloned.1.call-done = bf16[768,768]{1,0:T(8,128)(2,1)} async-done(((bf16[3072,768]{1,0:T(8,128)(2,1)}), bf16[768,768]{1,0:T(8,128)(2,1)}) %reduce-scatter.20.cloned.1.call-update) | async-done | bytes 1179664 | tf_op jit(solution)/shard_map/reduce_scatter | solution.py:165
  614.6 3.5 add_convert_fusion.3
  618.1 6.2 multiply_convert_fusion.3
  624.3 13.3 %reduce-scatter.22.cloned.1.call-done = bf16[192,2]{1,0:T(8,128)(2,1)} async-done(((bf16[768,2]{1,0:T(8,128)(2,1)}), bf16[192,2]{1,0:T(8,128)(2,1)}) %reduce-scatter.22.cloned.1.call-update) | async-done | bytes 784
  638.4 19.1 %reduce-scatter.24.cloned.1.call-done = bf16[192,2]{1,0:T(8,128)(2,1)} async-done(((bf16[768,2]{1,0:T(8,128)(2,1)}), bf16[192,2]{1,0:T(8,128)(2,1)}) %reduce-scatter.24.cloned.1.call-update) | async-done | bytes 784
  658.4 19.3 %reduce-scatter.26.cloned.1.call-done = bf16[192,2]{1,0:T(8,128)(2,1)} async-done(((bf16[768,2]{1,0:T(8,128)(2,1)}), bf16[192,2]{1,0:T(8,128)(2,1)}) %reduce-scatter.26.cloned.1.call-update) | async-done | bytes 784
  678.5 12.2 %all-reduce = (bf16[2,192]{1,0:T(2,128)(2,1)S(1)}, bf16[2,192]{1,0:T(2,128)(2,1)S(1)}, bf16[2,192]{1,0:T(2,128)(2,1)S(1)}) all-reduce(bf16[2,192]{1,0:T(2,128)(2,1)S(1)} %copy.84, bf16[2,192]{1,0:T(2,128)(2,1)S(1)} %copy.86, bf16[2,192]{1,0:T(2,128)(2,1)S(1)} %copy.88), channel_id=1, replica_groups=mesh['dp'=8,'fsdp'=4] {'dp'}, use_global_device_ids=true, to_apply=%region_32.33 | all-reduce | flops 1152 | bytes 4608 | tf_op jit(solution)/shard_map/psum | solution.py:183
  692.5 60.7 %all-reduce.4.cloned.1.call-done = (bf16[192,2304]{1,0:T(8,128)(2,1)}, bf16[192,768]{1,0:T(8,128)(2,1)}, bf16[192,3072]{1,0:T(8,128)(2,1)}, bf16[768,768]{1,0:T(8,128)(2,1)}) async-done(((bf16[192,2304]{1,0:T(8,128)(2,1)}, bf16[192,768]{1,0:T(8,128)(2,1)}, bf16[192,3072]{1,0:T(8,128)(2,1)}, bf16[768,768]{1,0:T(8,128)(2,1)}), (bf16[192,2304]{1,0:T(8,128)(2,1)}, bf16[192,768]{1,0:T(8,128)(2,1)}, ...) | async-done | bytes 3538960 | tf_op jit(solution)/shard_map/psum | solution.py:179
  753.2 1.9 convert_element_type.168
  755.1 2.5 convert_element_type.166
  757.6 1.7 convert_element_type.170
  759.3 1.6 convert_element_type.172
  (181 shorter events, 29.8 us)
Async XLA Ops:
  7.2 2.9 copy-start.36
  7.2 4.4 copy-start.32
  7.2 17.2 %copy-start.33 = (bf16[2,192]{1,0:T(2,128)(2,1)S(1)}, bf16[2,192]{1,0:T(2,128)(2,1)}, u32[]{:S(2)}) copy-start(bf16[2,192]{1,0:T(2,128)(2,1)} %param.17) | copy-start | bytes 2308
  7.2 25.3 %copy-start.34 = (bf16[2,192]{1,0:T(2,128)(2,1)S(1)}, bf16[2,192]{1,0:T(2,128)(2,1)}, u32[]{:S(2)}) copy-start(bf16[2,192]{1,0:T(2,128)(2,1)} %param.18) | copy-start | bytes 2308
  7.2 36.2 %copy-start.5 = (bf16[576,768]{1,0:T(8,128)(2,1)S(1)}, bf16[576,768]{1,0:T(8,128)(2,1)}, u32[]{:S(2)}) copy-start(bf16[576,768]{1,0:T(8,128)(2,1)} %param.10) | copy-start | bytes 2654212
  7.2 75.1 %all-gather.8.cloned.1.call-start = ((), (), s32[]{:S(2)}) async-start(), calls=%async_computation.7 | async-start | bytes 4423680 | tf_op jit(solution)/shard_map/all_gather | solution.py:33
  8.0 119.4 %all-gather.10.cloned.1.call-start = ((), (), s32[]{:S(2)}) async-start(), calls=%async_computation.8 | async-start | bytes 1474560 | tf_op jit(solution)/shard_map/all_gather | solution.py:34
  8.7 194.4 %all-gather.12.cloned.1.call-start = ((), (), s32[]{:S(2)}) async-start(), calls=%async_computation.9 | async-start | bytes 5898240 | tf_op jit(solution)/shard_map/all_gather | solution.py:35
  9.4 282.9 %all-gather.14.cloned.1.call-start = ((), (), s32[]{:S(2)}) async-start(), calls=%async_computation.10 | async-start | bytes 5898240 | tf_op jit(solution)/shard_map/all_gather | solution.py:36
  10.0 393.5 %reduce-scatter.16.cloned.1.call-start = ((), (), s32[]{:S(2)}) async-start(), calls=%async_computation.12 | async-start | bytes 1474560 | tf_op jit(solution)/shard_map/reduce_scatter | solution.py:159
  43.7 43.0 %copy-start.22 = (f32[576]{0:T(1024)}, f32[576]{0:T(1024)S(1)}, u32[]{:S(2)}) copy-start(f32[576]{0:T(1024)S(1)} %broadcast_multiply_fusion.5) | copy-start | bytes 6916
  44.1 42.6 %copy-start.24 = (f32[576]{0:T(1024)}, f32[576]{0:T(1024)S(1)}, u32[]{:S(2)}) copy-start(f32[576]{0:T(1024)S(1)} %fusion.28) | copy-start | bytes 6916
  44.1 42.6 %copy-start.28 = (f32[576]{0:T(1024)}, f32[576]{0:T(1024)S(1)}, u32[]{:S(2)}) copy-start(f32[576]{0:T(1024)S(1)} %fusion.49) | copy-start | bytes 6916
  44.5 42.2 %copy-start.26 = (f32[768]{0:T(1024)}, f32[768]{0:T(1024)S(1)}, u32[]{:S(2)}) copy-start(f32[768]{0:T(1024)S(1)} %get-tuple-element.101) | copy-start | bytes 9220
  44.5 42.2 %copy-start.30 = (f32[768]{0:T(1024)}, f32[768]{0:T(1024)S(1)}, u32[]{:S(2)}) copy-start(f32[768]{0:T(1024)S(1)} %get-tuple-element.74) | copy-start | bytes 9220
  97.2 2.2 copy-start
  292.3 11.3 %copy-start.8 = (f32[576,768]{1,0:T(8,128)S(1)}, f32[576,768]{1,0:T(8,128)}, u32[]{:S(2)}) copy-start(f32[576,768]{1,0:T(8,128)} %copy-done.7) | copy-start | bytes 5308420
  292.4 11.3 %copy-start.35 = (bf16[768,3072]{1,0:T(8,128)(2,1)S(1)}, bf16[768,3072]{1,0:T(8,128)(2,1)}, u32[]{:S(2)}) copy-start(bf16[768,3072]{1,0:T(8,128)(2,1)} %all-gather.12.cloned.1.call-done) | copy-start | bytes 14155780
  303.7 3.3 copy-start.38
  307.0 1.9 copy-start.12
  307.8 2.5 copy-start.37
  312.4 126.3 %reduce-scatter.14.cloned.1.call-start = ((), (), s32[]{:S(2)}) async-start(), calls=%async_computation.11 | async-start | bytes 4423680 | tf_op jit(solution)/shard_map/reduce_scatter | solution.py:156
  318.2 19.6 %slice-start = ((s8[17694720]{0:T(1024)(128)(4,1)}), s8[4194304]{0:T(1024)(128)(4,1)S(1)}, s32[]{:S(2)}) async-start(s8[17694720]{0:T(1024)(128)(4,1)} %bitcast.91), calls=%async_computation.19 | async-start | bytes 8388608
  318.2 19.6 %slice-start.1 = ((s8[17694720]{0:T(1024)(128)(4,1)}), s8[917504]{0:T(1024)(128)(4,1)S(1)}, s32[]{:S(2)}) async-start(s8[17694720]{0:T(1024)(128)(4,1)} %bitcast.91), calls=%async_computation.20 | async-start | bytes 1835008
  325.8 12.0 %slice-start.2 = ((s8[17694720]{0:T(1024)(128)(4,1)}), s8[4194304]{0:T(1024)(128)(4,1)S(1)}, s32[]{:S(2)}) async-start(s8[17694720]{0:T(1024)(128)(4,1)} %bitcast.91), calls=%async_computation.21 | async-start | bytes 8388608
  325.8 12.0 %slice-start.3 = ((s8[17694720]{0:T(1024)(128)(4,1)}), s8[4194304]{0:T(1024)(128)(4,1)S(1)}, s32[]{:S(2)}) async-start(s8[17694720]{0:T(1024)(128)(4,1)} %bitcast.91), calls=%async_computation.22 | async-start | bytes 8388608
  325.8 12.5 %slice-start.4 = ((s8[17694720]{0:T(1024)(128)(4,1)}), s8[4194304]{0:T(1024)(128)(4,1)S(1)}, s32[]{:S(2)}) async-start(s8[17694720]{0:T(1024)(128)(4,1)} %bitcast.91), calls=%async_computation.23 | async-start | bytes 8388608
  338.3 6.6 copy-start.1
  349.0 1.9 copy-start.2
  354.4 10.8 %copy-start.16 = (bf16[576,12,64]{0,2,1:T(8,128)(2,1)}, bf16[576,12,64]{0,2,1:T(8,128)(2,1)S(1)}, u32[]{:S(2)}) copy-start(bf16[576,12,64]{0,2,1:T(8,128)(2,1)S(1)} %add_convert_fusion.1) | copy-start | bytes 2654212
  354.4 1.6 copy-start.6
  355.9 9.2 %copy-start.18 = (bf16[576,12,64]{0,2,1:T(8,128)(2,1)}, bf16[576,12,64]{0,2,1:T(8,128)(2,1)S(1)}, u32[]{:S(2)}) copy-start(bf16[576,12,64]{0,2,1:T(8,128)(2,1)S(1)} %add_convert_fusion.2) | copy-start | bytes 2654212
  355.9 10.1 %copy-start.23 = (f32[576]{0:T(1024)S(1)}, f32[576]{0:T(1024)}, u32[]{:S(2)}) copy-start(f32[576]{0:T(1024)} %copy-done.22) | copy-start | bytes 6916
  355.9 10.1 %copy-start.27 = (f32[768]{0:T(1024)S(1)}, f32[768]{0:T(1024)}, u32[]{:S(2)}) copy-start(f32[768]{0:T(1024)} %copy-done.26) | copy-start | bytes 9220
  355.9 10.1 %copy-start.29 = (f32[576]{0:T(1024)S(1)}, f32[576]{0:T(1024)}, u32[]{:S(2)}) copy-start(f32[576]{0:T(1024)} %copy-done.28) | copy-start | bytes 6916
  355.9 10.1 %copy-start.31 = (f32[768]{0:T(1024)S(1)}, f32[768]{0:T(1024)}, u32[]{:S(2)}) copy-start(f32[768]{0:T(1024)} %copy-done.30) | copy-start | bytes 9220
  373.5 152.9 %reduce-scatter.18.cloned.1.call-start = ((), (), s32[]{:S(2)}) async-start(), calls=%async_computation.13 | async-start | bytes 5898240 | tf_op jit(solution)/shard_map/reduce_scatter | solution.py:162
  382.7 231.8 %reduce-scatter.20.cloned.1.call-start = ((), (), s32[]{:S(2)}) async-start(), calls=%async_computation.14 | async-start | bytes 5898240 | tf_op jit(solution)/shard_map/reduce_scatter | solution.py:165
  391.9 245.7 %reduce-scatter.22.cloned.1.call-start = ((), (), s32[]{:S(2)}) async-start(), calls=%async_computation.15 | async-start | bytes 245760
  393.4 5.0 copy-start.25
  401.4 256.1 %reduce-scatter.24.cloned.1.call-start = ((), (), s32[]{:S(2)}) async-start(), calls=%async_computation.16 | async-start | bytes 245760
  402.5 275.1 %reduce-scatter.26.cloned.1.call-start = ((), (), s32[]{:S(2)}) async-start(), calls=%async_computation.17 | async-start | bytes 245760
  402.6 212.0 %copy-start.4 = (f32[576,768]{1,0:T(8,128)S(1)}, f32[576,768]{1,0:T(8,128)}, u32[]{:S(2)}) copy-start(f32[576,768]{1,0:T(8,128)} %copy-done.3) | copy-start | bytes 5308420
  403.5 349.7 %all-reduce.4.cloned.1.call-start = ((), (), s32[]{:S(2)}) async-start(), calls=%async_computation.18 | async-start | bytes 7077888 | tf_op jit(solution)/shard_map/psum | solution.py:179
  614.6 3.5 copy-start.10
  614.6 3.5 copy-start.39
  753.2 4.4 copy-start.15
  757.6 1.7 copy-start.14
  (9 other events, 10.8 us)
Sparse Core Ops, SparseCore 0:
  9.6 72.6 all-gather.7
  83.9 28.9 all-gather.9
  114.4 88.6 all-gather.11
  204.5 87.7 all-gather.13
  312.5 27.7 reduce-scatter.15
  373.6 64.9 reduce-scatter.13
  440.9 85.4 reduce-scatter.17
  528.7 85.7 reduce-scatter.19
  617.4 20.1 reduce-scatter.21
  639.7 17.8 reduce-scatter.23
  659.8 17.8 reduce-scatter.25
  681.2 71.9 all-reduce.3
where the time goes:
time: 772 us; the launch traced here: 768 us
  waiting for transfers between devices  502 us (65%)
  matrix products  126 us (16%)
  other arithmetic  52.6 us (7%)
  blocking collectives  43.7 us (6%)
  local copies, waits for them, and re-layouts  27.9 us (4%)
  between operations  15.2 us (2%)
    reduce_scatter x1, waiting for transfers between devices, on_device(): lax.psum_scatter(summands[3].astype(jnp.bfloat16), 'fsdp', scatter_dimens...  88.1 us
    reduce_scatter x1, waiting for transfers between devices, on_device(): lax.psum_scatter(summands[2].astype(jnp.bfloat16), 'fsdp', scatter_dimens...  87.8 us
    all_gather x1, waiting for transfers between devices, on_device(): lax.all_gather(w_up, 'fsdp', axis=0, tiled=True)  71.6 us
    all_gather x1, waiting for transfers between devices, on_device(): lax.all_gather(w_down, 'fsdp', axis=0, tiled=True)  66.5 us
    psum x1, waiting for transfers between devices, on_device(): lax.psum(pieces[0].astype(jnp.bfloat16), 'dp').astype(jnp.float32)  60.7 us
    unnamed x15, waiting for transfers between devices  54.3 us
    all_gather x1, waiting for transfers between devices, on_device(): lax.all_gather(w_qkv, 'fsdp', axis=0, tiled=True)  37.8 us
    reduce_scatter x1, waiting for transfers between devices, on_device(): lax.psum_scatter(summands[0].astype(jnp.bfloat16), 'fsdp', scatter_dimens...  35.1 us
  transfers between devices with their start and end apart: 12, of which 10 were waited for; matrix products, arithmetic and copies ran while one was open for 22% of the time, Pallas kernels for 0%

commit v1 on v0

--- a/solution.py
+++ b/solution.py
@@ -8,6 +8,27 @@
 HEAD_DIM = 64
 PATCH_BIG = 576
 epsilon = 1e-06
+
+
+def ring_gather(array, axis, dim):
+    size, index, extent = (lax.axis_size(axis), lax.axis_index(axis), array.shape[dim])
+    upward = [(i, (i + 1) % size) for i in range(size)]
+    left = [(i, (i - 1) % size) for i in range(size)]
+    out = jnp.zeros((*array.shape[:dim], size * extent, *array.shape[dim + 1 :]), array.dtype)
+    out = lax.dynamic_update_slice_in_dim(out, array, index * extent, axis=dim)
+    from_left = from_right = array
+    half = size // 2
+    for lap in range(1, half + 1):
+        from_left = lax.ppermute(from_left, axis, upward)
+        out = lax.dynamic_update_slice_in_dim(
+            out, from_left, (index - lap) % size * extent, axis=dim
+        )
+        if lap < size - half:
+            from_right = lax.ppermute(from_right, axis, left)
+            out = lax.dynamic_update_slice_in_dim(
+                out, from_right, (index + lap) % size * extent, axis=dim
+            )
+    return out
 
 
 def layer_norm(v, gain_row, bias_row):
@@ -32,7 +53,7 @@
     full_qkv, full_out, full_up, full_down, gain_all, bias_all, qk_all = (
         lax.all_gather(w_qkv, "fsdp", axis=0, tiled=True),
         lax.all_gather(w_out, "fsdp", axis=0, tiled=True),
-        lax.all_gather(w_up, "fsdp", axis=0, tiled=True),
+        ring_gather(w_up, "fsdp", 0),
         lax.all_gather(w_down, "fsdp", axis=0, tiled=True),
         lax.all_gather(ln_gain, "fsdp", axis=1, tiled=True),
         lax.all_gather(ln_bias, "fsdp", axis=1, tiled=True),

time: 772 us -> 832 us (1.078)
  blocking collectives: 43.7 us -> 134 us
  waiting for transfers between devices: 502 us -> 445 us
  local copies, waits for them, and re-layouts: 27.9 us -> 38.2 us
    all_gather x1, blocking collectives: 8.07 us -> 102 us  [on_device(): lax.all_gather(ln_bias, 'fsdp', axis=1, tiled=True)]
    all_gather x1, waiting for transfers between devices: 66.5 us -> 6 us  [on_device(): lax.all_gather(w_down, 'fsdp', axis=0, tiled=True)]
    all_gather x1, waiting for transfers between devices: 37.8 us -> 0.01 us  [on_device(): lax.all_gather(w_qkv, 'fsdp', axis=0, tiled=True)]
    ppermute x0 -> x3, waiting for transfers between devices: none -> 31 us  [the longest x2 31 us: ring_gather(): from_left = lax.ppermute(from_left, axis, upward)]
  transfers between devices with their start and end apart: 12 -> 15, of which waited for: 10 -> 10; matrix products, arithmetic and copies ran while one was open for 22% -> 19% of each run, Pallas kernels for 0% -> 0%
where the time goes in v1:
time: 832 us; the launch traced here: 827 us
  waiting for transfers between devices  445 us (53%)
  blocking collectives  134 us (16%)
  matrix products  132 us (16%)
  other arithmetic  56.2 us (7%)
  local copies, waits for them, and re-layouts  38.2 us (5%)
  between operations  15.2 us (2%)
    all_gather x1, blocking collectives, on_device(): lax.all_gather(ln_bias, 'fsdp', axis=1, tiled=True)  102 us
    reduce_scatter x1, waiting for transfers between devices, on_device(): lax.psum_scatter(summands[2].astype(jnp.bfloat16), 'fsdp', scatter_dimens...  88.1 us
    reduce_scatter x1, waiting for transfers between devices, on_device(): lax.psum_scatter(summands[3].astype(jnp.bfloat16), 'fsdp', scatter_dimens...  87.8 us
    all_gather x1, waiting for transfers between devices, on_device(): lax.all_gather(w_up, 'fsdp', axis=0, tiled=True)  76.1 us
    psum x1, waiting for transfers between devices, on_device(): lax.psum(pieces[0].astype(jnp.bfloat16), 'dp').astype(jnp.float32)  60.7 us
    unnamed x15, waiting for transfers between devices  54.4 us
    reduce_scatter x1, waiting for transfers between devices, on_device(): lax.psum_scatter(summands[0].astype(jnp.bfloat16), 'fsdp', scatter_dimens...  41 us
    ppermute x2, waiting for transfers between devices, ring_gather(): from_left = lax.ppermute(from_left, axis, upward)  31 us
  transfers between devices with their start and end apart: 15, of which 10 were waited for; matrix products, arithmetic and copies ran while one was open for 19% of the time, Pallas kernels for 0%

profile of v1, /device:TPU:0, one launch (start us, length us, event | category | flops | bytes accessed | tf_op | source)
XLA Modules:
  0.0 826.6 jit_solution(15622052210760268302)
XLA Ops:
  9.5 3.1 collective-permute-start
  12.6 2.1 collective-permute-start.1
  14.9 101.7 %all-gather.1 = bf16[4,192,2]{1,2,0:T(2,128)(2,1)S(1)} all-gather(bf16[1,192,2]{1,2,0:T(2,128)(2,1)S(1)} %bitcast.126), channel_id=1, replica_groups=mesh['dp'=8,'fsdp'=4] {'fsdp'}, dimensions={0}, use_global_device_ids=true | all-gather | bytes 3840 | tf_op jit(solution)/shard_map/all_gather | solution.py:59
  116.7 10.2 %all-gather = bf16[4,192,2]{1,2,0:T(2,128)(2,1)S(1)} all-gather(bf16[1,192,2]{1,2,0:T(2,128)(2,1)S(1)} %bitcast.127), channel_id=1, replica_groups=mesh['dp'=8,'fsdp'=4] {'fsdp'}, dimensions={0}, use_global_device_ids=true | all-gather | bytes 3840 | tf_op jit(solution)/shard_map/all_gather | solution.py:58
  127.3 9.4 %all-gather.2 = bf16[4,192,2]{1,2,0:T(2,128)(2,1)S(1)} all-gather(bf16[1,192,2]{1,2,0:T(2,128)(2,1)S(1)} %bitcast.128), channel_id=1, replica_groups=mesh['dp'=8,'fsdp'=4] {'fsdp'}, dimensions={0}, use_global_device_ids=true | all-gather | bytes 3840 | tf_op jit(solution)/shard_map/all_gather | solution.py:60
  140.8 2.7 broadcast_in_dim.93
  144.7 2.4 constant_dynamic-update-slice_fusion.2
  147.1 2.4 constant_dynamic-update-slice_fusion.1
  149.5 31.0 %collective-permute-done.2 = bf16[192,3072]{1,0:T(8,128)(2,1)S(1)} collective-permute-done((bf16[192,3072]{1,0:T(8,128)(2,1)}, bf16[192,3072]{1,0:T(8,128)(2,1)S(1)}, u32[]{:S(2)}, u32[]{:S(2)}) %collective-permute-start.2) | collective-permute-done | bytes 1179680 | tf_op jit(solution)/shard_map/ppermute | solution.py:22
  181.6 4.4 fusion.54
  188.4 2.4 copy.68
  192.6 1.9 copy.69
  196.6 2.0 multiply_reduce_fusion
  198.7 8.1 fusion.62
  206.8 8.6 %fusion.3 = f32[12,576]{1,0:T(8,128)S(1)} fusion(f32[12,576,576]{1,2,0:T(8,128)} %get-tuple-element.91, f32[12,576]{1,0:T(8,128)S(1)} %get-tuple-element.90), kind=kLoop, calls=%fused_computation.9 | loop fusion | flops 7955712 | bytes 15980544 | tf_op jit(solution)/shard_map/while/body/eval_jaxpr/reduce_sum | solution.py:98
  215.4 10.7 %fusion.31 = bf16[12,64,576]{2,1,0:T(8,128)(2,1)} fusion(bf16[576,12,64]{0,2,1:T(8,128)(2,1)} %bitcast.109, f32[12,576,576]{1,2,0:T(8,128)} %get-tuple-element.91, f32[12,576]{1,0:T(8,128)S(1)} %fusion.3, f32[12,576]{1,0:T(8,128)S(1)} %get-tuple-element.90), kind=kOutput, calls=%fused_computation.81 | convolution fusion | flops 521994240 | bytes 17750016 | tf_op jit(solution)/shard_map/while/body/eval_jaxpr/hqk,khd->qhd/dot_general | solution.py:100
  226.1 2.6 fusion.63
  229.9 22.0 %multiply_convert_fusion = (bf16[576,3072]{1,0:T(8,128)(2,1)}, f32[576,3072]{1,0:T(8,128)}, f32[576,3072]{1,0:T(8,128)}) fusion(bf16[768,3072]{1,0:T(8,128)(2,1)} %constant_dynamic-update-slice_fusion, f32[576,768]{1,0:T(8,128)S(1)} %get-tuple-element.93, f32[768]{0:T(1024)S(1)} %get-tuple-element.73, f32[768]{0:T(1024)S(1)} %get-tuple-element.71, ...), kind=kOutput, calls=%fused_computation.17 | convolution fusion | flops 2835136512 | bytes 24193536 | tf_op jit(solution)/shard_map/dot_general | solution.py:110
  251.9 6.0 all-gather.12.cloned.1.call-done
  257.9 13.1 %add_convert_fusion = bf16[576,3072]{1,0:T(8,128)(2,1)} fusion(f32[576,3072]{1,0:T(8,128)} %get-tuple-element.87, f32[576,3072]{1,0:T(8,128)} %get-tuple-element.94, bf16[3072,768]{1,0:T(8,128)(2,1)} %all-gather.12.cloned.1.call-done, bf16[576,768]{1,0:T(8,128)(2,1)} %param.19, f32[576]{0:T(1024)S(1)} %fusion.48), kind=kOutput, calls=%fused_computation.16 | convolution fusion | flops 2744008704 | bytes 23300352 | tf_op jit(solution)/shard_map/dot_general | solution.py:124
  271.0 76.1 %all-gather.14.cloned.1.call-done = bf16[768,3072]{1,0:T(8,128)(2,1)} async-done(((bf16[192,3072]{1,0:T(8,128)(2,1)}), bf16[768,3072]{1,0:T(8,128)(2,1)}) %all-gather.14.cloned.1.call-update) | async-done | bytes 4718608 | tf_op jit(solution)/shard_map/all_gather | solution.py:118
  347.1 7.3 multiply_reduce_fusion.2
  357.6 2.1 convolution_convert_fusion.4
  359.8 3.3 convolution_convert_fusion.5
  363.1 2.2 copy.73
  365.3 7.6 convolution_convert_fusion
  373.0 12.8 %fusion = f32[12,576]{1,0:T(8,128)S(1)} fusion(bf16[12,576,576]{1,2,0:T(8,128)(2,1)} %convolution_convert_fusion, f32[12,576,576]{1,2,0:T(8,128)} %get-tuple-element.91, f32[12,576]{1,0:T(8,128)S(1)} %log_add_fusion), kind=kLoop, calls=%fused_computation.2 | loop fusion | flops 15918336 | bytes 23943168 | tf_op jit(solution)/shard_map/while/body/eval_jaxpr/reduce_sum | solution.py:144
  385.8 6.6 fusion.2
  392.5 4.0 fusion.23
  396.5 2.8 fusion.21
  399.3 3.1 fusion.24
  402.6 2.9 fusion.22
  408.6 9.1 %fusion.32 = bf16[12,64,576]{2,1,0:T(8,128)(2,1)S(1)} fusion(bf16[576,12,64]{0,2,1:T(8,128)(2,1)S(1)} %bitcast.108, f32[12,576,576]{1,2,0:T(8,128)} %get-tuple-element.91, f32[12,576]{1,0:T(8,128)S(1)} %log_add_fusion), kind=kOutput, calls=%fused_computation.82 | convolution fusion | flops 518012928 | bytes 17722368 | tf_op jit(solution)/shard_map/while/body/eval_jaxpr/hqk,qhd->khd/dot_general | solution.py:141
  418.7 7.3 convolution_convert_fusion.1
  427.2 8.0 convolution_convert_fusion.2
  436.7 8.2 convolution_convert_fusion.3
  446.5 5.0 fusion.58
  456.7 41.0 %reduce-scatter.14.cloned.1.call-done = bf16[192,2304]{1,0:T(8,128)(2,1)} async-done(((bf16[768,2304]{1,0:T(8,128)(2,1)}), bf16[192,2304]{1,0:T(8,128)(2,1)}) %reduce-scatter.14.cloned.1.call-update) | async-done | bytes 884752 | tf_op jit(solution)/shard_map/reduce_scatter | solution.py:177
  497.7 87.8 %reduce-scatter.20.cloned.1.call-done = bf16[768,768]{1,0:T(8,128)(2,1)} async-done(((bf16[3072,768]{1,0:T(8,128)(2,1)}), bf16[768,768]{1,0:T(8,128)(2,1)}) %reduce-scatter.20.cloned.1.call-update) | async-done | bytes 1179664 | tf_op jit(solution)/shard_map/reduce_scatter | solution.py:186
  585.5 88.1 %reduce-scatter.18.cloned.1.call-done = bf16[192,3072]{1,0:T(8,128)(2,1)} async-done(((bf16[768,3072]{1,0:T(8,128)(2,1)}), bf16[192,3072]{1,0:T(8,128)(2,1)}) %reduce-scatter.18.cloned.1.call-update) | async-done | bytes 1179664 | tf_op jit(solution)/shard_map/reduce_scatter | solution.py:183
  673.7 3.5 add_convert_fusion.3
  677.1 6.2 multiply_convert_fusion.3
  683.3 13.3 %reduce-scatter.22.cloned.1.call-done = bf16[192,2]{1,0:T(8,128)(2,1)} async-done(((bf16[768,2]{1,0:T(8,128)(2,1)}), bf16[192,2]{1,0:T(8,128)(2,1)}) %reduce-scatter.22.cloned.1.call-update) | async-done | bytes 784
  697.5 19.7 %reduce-scatter.24.cloned.1.call-done = bf16[192,2]{1,0:T(8,128)(2,1)} async-done(((bf16[768,2]{1,0:T(8,128)(2,1)}), bf16[192,2]{1,0:T(8,128)(2,1)}) %reduce-scatter.24.cloned.1.call-update) | async-done | bytes 784
  718.0 19.3 %reduce-scatter.26.cloned.1.call-done = bf16[192,2]{1,0:T(8,128)(2,1)} async-done(((bf16[768,2]{1,0:T(8,128)(2,1)}), bf16[192,2]{1,0:T(8,128)(2,1)}) %reduce-scatter.26.cloned.1.call-update) | async-done | bytes 784
  738.1 12.2 %all-reduce = (bf16[2,192]{1,0:T(2,128)(2,1)S(1)}, bf16[2,192]{1,0:T(2,128)(2,1)S(1)}, bf16[2,192]{1,0:T(2,128)(2,1)S(1)}) all-reduce(bf16[2,192]{1,0:T(2,128)(2,1)S(1)} %copy.84, bf16[2,192]{1,0:T(2,128)(2,1)S(1)} %copy.86, bf16[2,192]{1,0:T(2,128)(2,1)S(1)} %copy.88), channel_id=1, replica_groups=mesh['dp'=8,'fsdp'=4] {'dp'}, use_global_device_ids=true, to_apply=%region_32.33 | all-reduce | flops 1152 | bytes 4608 | tf_op jit(solution)/shard_map/psum | solution.py:204
  752.1 60.7 %all-reduce.4.cloned.1.call-done = (bf16[192,2304]{1,0:T(8,128)(2,1)}, bf16[192,768]{1,0:T(8,128)(2,1)}, bf16[192,3072]{1,0:T(8,128)(2,1)}, bf16[768,768]{1,0:T(8,128)(2,1)}) async-done(((bf16[192,2304]{1,0:T(8,128)(2,1)}, bf16[192,768]{1,0:T(8,128)(2,1)}, bf16[192,3072]{1,0:T(8,128)(2,1)}, bf16[768,768]{1,0:T(8,128)(2,1)}), (bf16[192,2304]{1,0:T(8,128)(2,1)}, bf16[192,768]{1,0:T(8,128)(2,1)}, ...) | async-done | bytes 3538960 | tf_op jit(solution)/shard_map/psum | solution.py:200
  812.8 2.6 convert_element_type.166
  (200 shorter events, 41.8 us)
Async XLA Ops:
  7.2 7.7 copy-start.38
  7.2 109.5 %copy-start.39 = (bf16[2,192]{1,0:T(2,128)(2,1)S(1)}, bf16[2,192]{1,0:T(2,128)(2,1)}, u32[]{:S(2)}) copy-start(bf16[2,192]{1,0:T(2,128)(2,1)} %param.16) | copy-start | bytes 2308
  7.2 119.9 %copy-start.7 = (bf16[576,768]{1,0:T(8,128)(2,1)S(1)}, bf16[576,768]{1,0:T(8,128)(2,1)}, u32[]{:S(2)}) copy-start(bf16[576,768]{1,0:T(8,128)(2,1)} %param.10) | copy-start | bytes 2654212
  7.2 174.3 %all-gather.8.cloned.1.call-start = ((), (), s32[]{:S(2)}) async-start(), calls=%async_computation.7 | async-start | bytes 4423680 | tf_op jit(solution)/shard_map/all_gather | solution.py:54
  8.0 119.3 %copy-start.40 = (bf16[2,192]{1,0:T(2,128)(2,1)S(1)}, bf16[2,192]{1,0:T(2,128)(2,1)}, u32[]{:S(2)}) copy-start(bf16[2,192]{1,0:T(2,128)(2,1)} %param.18) | copy-start | bytes 2308
  8.0 129.0 %copy-start.41 = (s32[1,9]{1,0:T(1,128)S(1)}, s32[1,9]{1,0:T(1,128)}, u32[]{:S(2)}) copy-start(s32[1,9]{1,0:T(1,128)} %param.11) | copy-start | bytes 112
  8.0 218.2 %all-gather.10.cloned.1.call-start = ((), (), s32[]{:S(2)}) async-start(), calls=%async_computation.8 | async-start | bytes 1474560 | tf_op jit(solution)/shard_map/all_gather | solution.py:55
  8.7 249.1 %all-gather.12.cloned.1.call-start = ((), (), s32[]{:S(2)}) async-start(), calls=%async_computation.9 | async-start | bytes 5898240 | tf_op jit(solution)/shard_map/all_gather | solution.py:57
  9.5 337.7 %all-gather.14.cloned.1.call-start = ((), (), s32[]{:S(2)}) async-start(), calls=%async_computation.10 | async-start | bytes 5898240 | tf_op jit(solution)/shard_map/all_gather | solution.py:118
  9.5 130.3 %collective-permute-start = (bf16[192,3072]{1,0:T(8,128)(2,1)S(1)}, bf16[192,3072]{1,0:T(8,128)(2,1)}, u32[]{:S(2)}, u32[]{:S(2)}) collective-permute-start(bf16[192,3072]{1,0:T(8,128)(2,1)S(1)} %copy-done.14), channel_id=1, source_target_pairs={{0,1},{1,2},{2,3},{3,0},{4,5},{5,6},{6,7},{7,4},{8,9},{9,10},{10,1... | collective-permute-start | bytes 3538952 | tf_op jit(solution)/shard_map/ppermute | solution.py:22
  12.6 134.5 %collective-permute-start.1 = (bf16[192,3072]{1,0:T(8,128)(2,1)S(1)}, bf16[192,3072]{1,0:T(8,128)(2,1)}, u32[]{:S(2)}, u32[]{:S(2)}) collective-permute-start(bf16[192,3072]{1,0:T(8,128)(2,1)S(1)} %copy-done.14), channel_id=1, source_target_pairs={{0,3},{1,0},{2,1},{3,2},{4,7},{5,4},{6,5},{7,6},{8,11},{9,8},{10,9... | collective-permute-start | bytes 3538952 | tf_op jit(solution)/shard_map/ppermute | solution.py:27
  14.7 442.0 %reduce-scatter.16.cloned.1.call-start = ((), (), s32[]{:S(2)}) async-start(), calls=%async_computation.12 | async-start | bytes 1474560 | tf_op jit(solution)/shard_map/reduce_scatter | solution.py:180
  116.7 64.9 %copy-start.36 = (f32[768]{0:T(1024)}, f32[768]{0:T(1024)S(1)}, u32[]{:S(2)}) copy-start(f32[768]{0:T(1024)S(1)} %get-tuple-element.74) | copy-start | bytes 9220
  127.3 54.3 %copy-start.28 = (f32[576]{0:T(1024)}, f32[576]{0:T(1024)S(1)}, u32[]{:S(2)}) copy-start(f32[576]{0:T(1024)S(1)} %broadcast_multiply_fusion.5) | copy-start | bytes 6916
  138.9 42.7 %copy-start.34 = (f32[576]{0:T(1024)}, f32[576]{0:T(1024)S(1)}, u32[]{:S(2)}) copy-start(f32[576]{0:T(1024)S(1)} %fusion.49) | copy-start | bytes 6916
  139.5 42.1 %copy-start.32 = (f32[768]{0:T(1024)}, f32[768]{0:T(1024)S(1)}, u32[]{:S(2)}) copy-start(f32[768]{0:T(1024)S(1)} %get-tuple-element.72) | copy-start | bytes 9220
  139.8 40.7 %collective-permute-start.2 = (bf16[192,3072]{1,0:T(8,128)(2,1)}, bf16[192,3072]{1,0:T(8,128)(2,1)S(1)}, u32[]{:S(2)}, u32[]{:S(2)}) collective-permute-start(bf16[192,3072]{1,0:T(8,128)(2,1)} %collective-permute-done), channel_id=1, source_target_pairs={{0,1},{1,2},{2,3},{3,0},{4,5},{5,6},{6,7},{7,4},{8,9},{9,10},{10,1... | collective-permute-start | bytes 3538952 | tf_op jit(solution)/shard_map/ppermute | solution.py:22
  140.8 2.7 copy-start.15
  347.1 7.3 copy-start.10
  355.2 2.5 copy-start.42
  365.3 20.4 %slice-start = ((s8[17694720]{0:T(1024)(128)(4,1)}), s8[4194304]{0:T(1024)(128)(4,1)S(1)}, s32[]{:S(2)}) async-start(s8[17694720]{0:T(1024)(128)(4,1)} %bitcast.91), calls=%async_computation.19 | async-start | bytes 8388608
  365.3 20.4 %slice-start.1 = ((s8[17694720]{0:T(1024)(128)(4,1)}), s8[917504]{0:T(1024)(128)(4,1)S(1)}, s32[]{:S(2)}) async-start(s8[17694720]{0:T(1024)(128)(4,1)} %bitcast.91), calls=%async_computation.20 | async-start | bytes 1835008
  373.0 12.8 %slice-start.2 = ((s8[17694720]{0:T(1024)(128)(4,1)}), s8[4194304]{0:T(1024)(128)(4,1)S(1)}, s32[]{:S(2)}) async-start(s8[17694720]{0:T(1024)(128)(4,1)} %bitcast.91), calls=%async_computation.21 | async-start | bytes 8388608
  373.0 12.8 %slice-start.3 = ((s8[17694720]{0:T(1024)(128)(4,1)}), s8[4194304]{0:T(1024)(128)(4,1)S(1)}, s32[]{:S(2)}) async-start(s8[17694720]{0:T(1024)(128)(4,1)} %bitcast.91), calls=%async_computation.22 | async-start | bytes 8388608
  373.0 12.8 %slice-start.4 = ((s8[17694720]{0:T(1024)(128)(4,1)}), s8[4194304]{0:T(1024)(128)(4,1)S(1)}, s32[]{:S(2)}) async-start(s8[17694720]{0:T(1024)(128)(4,1)} %bitcast.91), calls=%async_computation.23 | async-start | bytes 8388608
  385.8 6.7 copy-start.1
  396.5 2.8 copy-start.27
  402.5 95.2 %reduce-scatter.14.cloned.1.call-start = ((), (), s32[]{:S(2)}) async-start(), calls=%async_computation.11 | async-start | bytes 4423680 | tf_op jit(solution)/shard_map/reduce_scatter | solution.py:177
  402.5 2.9 copy-start.2
  402.5 2.9 copy-start.4
  407.0 10.8 %copy-start.20 = (bf16[576,12,64]{0,2,1:T(8,128)(2,1)}, bf16[576,12,64]{0,2,1:T(8,128)(2,1)S(1)}, u32[]{:S(2)}) copy-start(bf16[576,12,64]{0,2,1:T(8,128)(2,1)S(1)} %add_convert_fusion.1) | copy-start | bytes 2654212
  408.6 9.2 %copy-start.22 = (bf16[576,12,64]{0,2,1:T(8,128)(2,1)}, bf16[576,12,64]{0,2,1:T(8,128)(2,1)S(1)}, u32[]{:S(2)}) copy-start(bf16[576,12,64]{0,2,1:T(8,128)(2,1)S(1)} %add_convert_fusion.2) | copy-start | bytes 2654212
  408.6 10.1 %copy-start.29 = (f32[576]{0:T(1024)S(1)}, f32[576]{0:T(1024)}, u32[]{:S(2)}) copy-start(f32[576]{0:T(1024)} %copy-done.28) | copy-start | bytes 6916
  408.6 10.1 %copy-start.33 = (f32[768]{0:T(1024)S(1)}, f32[768]{0:T(1024)}, u32[]{:S(2)}) copy-start(f32[768]{0:T(1024)} %copy-done.32) | copy-start | bytes 9220
  408.6 10.1 %copy-start.35 = (f32[576]{0:T(1024)S(1)}, f32[576]{0:T(1024)}, u32[]{:S(2)}) copy-start(f32[576]{0:T(1024)} %copy-done.34) | copy-start | bytes 6916
  408.6 10.1 %copy-start.37 = (f32[768]{0:T(1024)S(1)}, f32[768]{0:T(1024)}, u32[]{:S(2)}) copy-start(f32[768]{0:T(1024)} %copy-done.36) | copy-start | bytes 9220
  426.1 159.4 %reduce-scatter.20.cloned.1.call-start = ((), (), s32[]{:S(2)}) async-start(), calls=%async_computation.14 | async-start | bytes 5898240 | tf_op jit(solution)/shard_map/reduce_scatter | solution.py:186
  435.3 238.3 %reduce-scatter.18.cloned.1.call-start = ((), (), s32[]{:S(2)}) async-start(), calls=%async_computation.13 | async-start | bytes 5898240 | tf_op jit(solution)/shard_map/reduce_scatter | solution.py:183
  445.0 251.6 %reduce-scatter.22.cloned.1.call-start = ((), (), s32[]{:S(2)}) async-start(), calls=%async_computation.15 | async-start | bytes 245760
  446.5 5.0 copy-start.31
  454.6 262.6 %reduce-scatter.24.cloned.1.call-start = ((), (), s32[]{:S(2)}) async-start(), calls=%async_computation.16 | async-start | bytes 245760
  455.7 281.6 %reduce-scatter.26.cloned.1.call-start = ((), (), s32[]{:S(2)}) async-start(), calls=%async_computation.17 | async-start | bytes 245760
  455.7 217.9 %copy-start.6 = (f32[576,768]{1,0:T(8,128)S(1)}, f32[576,768]{1,0:T(8,128)}, u32[]{:S(2)}) copy-start(f32[576,768]{1,0:T(8,128)} %copy-done.5) | copy-start | bytes 5308420
  456.6 356.2 %all-reduce.4.cloned.1.call-start = ((), (), s32[]{:S(2)}) async-start(), calls=%async_computation.18 | async-start | bytes 7077888 | tf_op jit(solution)/shard_map/psum | solution.py:200
  673.6 3.5 copy-start.12
  673.7 3.5 copy-start.43
  812.8 2.6 copy-start.26
  812.8 3.5 copy-start.19
  (16 other events, 22.8 us)
Sparse Core Ops, SparseCore 0:
  9.6 113.5 all-gather.7
  124.7 41.5 all-gather.9
  167.9 89.9 all-gather.11
  259.3 87.7 all-gather.13
  402.6 27.7 reduce-scatter.15
  432.5 65.0 reduce-scatter.13
  500.0 85.4 reduce-scatter.19
  587.8 85.7 reduce-scatter.17
  676.4 20.1 reduce-scatter.21
  699.3 17.8 reduce-scatter.23
  719.4 17.8 reduce-scatter.25
  740.8 71.9 all-reduce.3
